TPU v7x, 512 devices: a whole 4x8x8 slice. The times are simulated.
512 devices in a mesh: row: 16 (over y, core), col: 32 (over z, x).
Axes of the slice: x: 4, y: 8, z: 8, core: 2. Of those that a mesh axis runs over, the one named last changes fastest.
Arguments:
- tokens: bfloat16 [1024, 8192], P('col', 'row'), may hold values from -6 to 6
- gate_weight: bfloat16 [8192, 16384], P('row', 'col'), may hold values from -0.09375 to 0.09375
- up_weight: bfloat16 [8192, 16384], P('row', 'col'), may hold values from -0.09375 to 0.09375
- down_weight: bfloat16 [16384, 8192], P('col', 'row'), may hold values from -0.0625 to 0.0625
- gate_mask: int32 [64, 128], P('row', 'col'), may hold values from 0 to 1, as said below
- up_mask: int32 [64, 128], P('row', 'col'), may hold values from 0 to 1, as said below
- down_mask: int32 [128, 64], P('col', 'row'), may hold values from 0 to 1, as said below
Outputs:
- mixed: bfloat16 [1024, 8192], P('col', 'row')
Inputs may be any that keep to these rules, and one draw needn't show every extreme that they name: `gate_mask`: each entry is 0 or 1; the share of ones differs from one block column of hidden units to another. `up_mask`: each entry is 0 or 1; the share of ones differs from one block column of hidden units to another. `down_mask`: each entry is 0 or 1; the share of ones differs from one block row of hidden units to another.
All inputs are finite; a program needn't handle non-finite values.
Results may differ from a plain program's by a relative error of at most 0.0049.
Values may be sent and summed in bfloat16 or wider, within the bound.
No kernel may reach another device: no remote copies, remote signals or barrier semaphores. Data moves between devices by JAX's collectives and lax.ppermute only.
A program may use at most 64 MiB of HBM per device.

v0:
```python
import jax
import jax.numpy as jnp
from jax import lax
from jax.sharding import Mesh
from jax.sharding import PartitionSpec as P

BLK = 128
ROW = ("y", "c")
COL = ("z", "x")


def widen(block_mask):
    rows_blocks, cols_blocks = block_mask.shape
    spread = jnp.broadcast_to(block_mask[:, None, :, None], (rows_blocks, BLK, cols_blocks, BLK))
    return spread.reshape(rows_blocks * BLK, cols_blocks * BLK).astype(jnp.bfloat16)


def swiglu(summed, hidden_cols):
    return (jax.nn.silu(summed[:, :hidden_cols]) * summed[:, hidden_cols:]).astype(jnp.bfloat16)


def gather_rows(x, axes):
    for axis in reversed(axes):
        x = lax.all_gather(x, axis, axis=0, tiled=True)
    return x


def on_device(tokens, gate_weight, up_weight, down_weight, gate_mask, up_mask, down_mask):
    hidden_cols = gate_weight.shape[1]
    both_weights = jnp.concatenate(
        [gate_weight * widen(gate_mask), up_weight * widen(up_mask)], axis=1
    )
    down_eff = down_weight * widen(down_mask)
    all_tokens = gather_rows(tokens, COL)
    n_y, n_c = (lax.axis_size("y"), lax.axis_size("c"))
    rows, feats = all_tokens.shape
    share = rows // (n_y * n_c)
    by_core = all_tokens.reshape(n_y, n_c, share, feats).transpose(1, 0, 2, 3).reshape(rows, feats)
    partial = jnp.dot(by_core, both_weights, preferred_element_type=jnp.float32)
    partial = lax.psum_scatter(partial, "c", scatter_dimension=0, tiled=True)
    summed = lax.psum_scatter(partial, "y", scatter_dimension=0, tiled=True)
    hidden_share = swiglu(summed, hidden_cols)
    hidden = gather_rows(hidden_share, ROW)
    partial_out = jnp.dot(hidden, down_eff, preferred_element_type=jnp.float32)
    for axis in COL:
        partial_out = lax.psum_scatter(partial_out, axis, scatter_dimension=0, tiled=True)
    return partial_out.astype(jnp.bfloat16)


def solution(mesh):
    n_row, n_col = mesh.devices.shape
    n_c = 2
    n_x = 4
    sub = Mesh(mesh.devices.reshape(n_row // n_c, n_c, n_col // n_x, n_x), ROW + COL)
    placed = (
        P(COL, ROW),
        P(ROW, COL),
        P(ROW, COL),
        P(COL, ROW),
        P(ROW, COL),
        P(ROW, COL),
        P(COL, ROW),
    )
    return jax.shard_map(
        on_device, mesh=sub, in_specs=placed, out_specs=P(COL, ROW), check_vma=False
    )
```

profile of v0, /device:TPU:8, one launch (start us, length us, event | category | flops | bytes accessed | tf_op | source)
XLA Modules:
  0.0 265.3 jit_solution(16039085546751924385)
XLA Ops:
  6.5 13.8 %all_gather.12 = bf16[128,512]{1,0:T(8,128)(2,1)} all-gather(bf16[32,512]{1,0:T(8,128)(2,1)} %param.7), channel_id=1, replica_groups=mesh['y'=8,'c'=2,'z'=8,'x'=4] {'x'}, dimensions={0}, use_global_device_ids=true | all-gather | bytes 163840 | tf_op jit(solution)/shard_map/all_gather | solution.py:24
  20.4 0.0 reduce-scatter.7.cloned.1.call-start
  20.4 0.7 convert_element_type.29
  21.1 0.7 convert_element_type.27
  21.8 0.2 broadcast_in_dim.7
  22.0 0.2 broadcast_in_dim.6
  22.2 1.4 bitcast_multiply_fusion.2
  23.6 42.3 %all-gather.3.cloned.1.call-done = bf16[1024,512]{1,0:T(8,128)(2,1)} async-done(((bf16[128,512]{1,0:T(8,128)(2,1)}), bf16[1024,512]{1,0:T(8,128)(2,1)}) %all-gather.3.cloned.1.call-update) | async-done | bytes 1048592 | tf_op jit(solution)/shard_map/all_gather | solution.py:24
  65.8 1.3 copy.11
  67.2 3.3 %convolution_bitcast_fusion = f32[1024,1024]{0,1:T(8,128)} fusion(bf16[1024,512]{1,0:T(8,128)(2,1)S(1)} %bitcast.26, bf16[512,512]{1,0:T(8,128)(2,1)S(1)} %get-tuple-element.5, bf16[512,512]{1,0:T(8,128)(2,1)S(1)} %get-tuple-element.6), kind=kOutput, calls=%fused_computation | convolution fusion | flops 1075838976 | bytes 6291456 | tf_op jit(solution)/shard_map/dot_general | solution.py:39
  70.4 0.0 reduce-scatter.13.cloned.1.call-start
  70.5 18.3 %reduce-scatter.7.cloned.1.call-done = f32[512,1024]{0,1:T(8,128)} async-done(((f32[1024,1024]{0,1:T(8,128)}), f32[512,1024]{0,1:T(8,128)}) %reduce-scatter.7.cloned.1.call-update) | async-done | bytes 2097168 | tf_op jit(solution)/shard_map/reduce_scatter | solution.py:40
  88.8 2.9 %copy.14 = f32[512,1024]{1,0:T(8,128)} copy(f32[512,1024]{0,1:T(8,128)} %reduce-scatter.7.cloned.1.call-done) | data formatting | bytes 4194304
  91.7 0.0 all-gather.5.cloned.1.call-start
  91.8 46.0 %reduce-scatter.13.cloned.1.call-done = f32[64,1024]{1,0:T(8,128)} async-done(((f32[512,1024]{1,0:T(8,128)}), f32[64,1024]{1,0:T(8,128)}) %reduce-scatter.13.cloned.1.call-update) | async-done | bytes 262160 | tf_op jit(solution)/shard_map/reduce_scatter | solution.py:41
  137.8 1.0 fusion.5
  138.8 2.0 all_gather.14
  140.8 0.0 reduce-scatter.9.cloned.1.call-start
  140.9 40.2 %all-gather.5.cloned.1.call-done = bf16[1024,512]{1,0:T(8,128)(2,1)} async-done(((bf16[128,512]{1,0:T(8,128)(2,1)}), bf16[1024,512]{1,0:T(8,128)(2,1)}) %all-gather.5.cloned.1.call-update) | async-done | bytes 1048592 | tf_op jit(solution)/shard_map/all_gather | solution.py:24
  181.1 0.2 broadcast_in_dim.8
  181.4 3.3 %fusion.3 = f32[1024,512]{1,0:T(8,128)} fusion(bf16[1024,512]{1,0:T(8,128)(2,1)} %all-gather.5.cloned.1.call-done, bf16[512,512]{1,0:T(8,128)(2,1)S(1)} %copy-done, bf16[64,8,4,128]{3,2,1,0:T(4,128)(2,1)S(1)} %bitcast.24), kind=kOutput, calls=%fused_computation.5 | convolution fusion | flops 537133056 | bytes 4194304 | tf_op jit(solution)/shard_map/dot_general | solution.py:44
  184.7 45.6 %reduce-scatter.9.cloned.1.call-done = f32[128,512]{1,0:T(8,128)} async-done(((f32[1024,512]{1,0:T(8,128)}), f32[128,512]{1,0:T(8,128)}) %reduce-scatter.9.cloned.1.call-update) | async-done | bytes 262160 | tf_op jit(solution)/shard_map/reduce_scatter | solution.py:46
  230.3 26.7 %reduce-scatter.11.cloned.1.call-done = f32[32,512]{1,0:T(8,128)} async-done(((f32[128,512]{1,0:T(8,128)}), f32[32,512]{1,0:T(8,128)}) %reduce-scatter.11.cloned.1.call-update) | async-done | bytes 65552 | tf_op jit(solution)/shard_map/reduce_scatter | solution.py:46
  257.0 1.5 convert_element_type.34
  (13 shorter events, 0.2 us)
Async XLA Ops:
  6.5 59.3 %all-gather.3.cloned.1.call-start = ((), (), s32[]{:S(2)}) async-start(), calls=%async_computation.4 | async-start | bytes 1179648 | tf_op jit(solution)/shard_map/all_gather | solution.py:24
  20.4 68.4 %reduce-scatter.7.cloned.1.call-start = ((), (), s32[]{:S(2)}) async-start(), calls=%async_computation.5 | async-start | bytes 6291456 | tf_op jit(solution)/shard_map/reduce_scatter | solution.py:40
  70.4 67.3 %reduce-scatter.13.cloned.1.call-start = ((), (), s32[]{:S(2)}) async-start(), calls=%async_computation.9 | async-start | bytes 2359296 | tf_op jit(solution)/shard_map/reduce_scatter | solution.py:41
  91.7 49.2 %copy-start.1 = (s32[4,4]{1,0:T(4,128)S(1)}, s32[4,4]{1,0:T(4,128)}, u32[]{:S(2)}) copy-start(s32[4,4]{1,0:T(4,128)} %param.13) | copy-start | bytes 196
  91.7 89.6 %copy-start = (bf16[512,512]{1,0:T(8,128)(2,1)S(1)}, bf16[512,512]{1,0:T(8,128)(2,1)}, u32[]{:S(2)}) copy-start(bf16[512,512]{1,0:T(8,128)(2,1)} %param.10) | copy-start | bytes 1572868
  91.7 89.4 %all-gather.5.cloned.1.call-start = ((), (), s32[]{:S(2)}) async-start(), calls=%async_computation.6 | async-start | bytes 1179648 | tf_op jit(solution)/shard_map/all_gather | solution.py:24
  140.8 89.4 %reduce-scatter.9.cloned.1.call-start = ((), (), s32[]{:S(2)}) async-start(), calls=%async_computation.7 | async-start | bytes 2359296 | tf_op jit(solution)/shard_map/reduce_scatter | solution.py:46
  184.7 72.3 %reduce-scatter.11.cloned.1.call-start = ((), (), s32[]{:S(2)}) async-start(), calls=%async_computation.8 | async-start | bytes 327680 | tf_op jit(solution)/shard_map/reduce_scatter | solution.py:46
Sparse Core Ops, SparseCore 0:
  20.5 45.2 all-gather.2
  70.6 18.1 reduce-scatter.6
  91.8 45.8 reduce-scatter.12
  141.0 40.1 all-gather.4
  184.8 45.4 reduce-scatter.8
  232.9 23.9 reduce-scatter.10
where the time goes:
time: 266 us; the launch traced here: 265 us
  waiting for transfers between devices  219 us (82%)
  blocking collectives  15.8 us (6%)
  between operations  13.5 us (5%)
  matrix products  6.54 us (2%)
  other arithmetic  5.21 us (2%)
  local copies, waits for them, and re-layouts  4.87 us (2%)
    all_gather x2, waiting for transfers between devices, gather_rows(): x = lax.all_gather(x, axis, axis=0, tiled=True)  82.5 us
    reduce_scatter x2, waiting for transfers between devices, on_device(): lax.psum_scatter(partial_out, axis, scatter_dimension=0, tiled=True)  72.2 us
    reduce_scatter x1, waiting for transfers between devices, on_device(): summed = lax.psum_scatter(partial, 'y', scatter_dimension=0, tiled=True)  46 us
    reduce_scatter x1, waiting for transfers between devices, on_device(): partial = lax.psum_scatter(partial, 'c', scatter_dimension=0, tiled=True)  18.3 us
    all_gather x2, blocking collectives, gather_rows(): x = lax.all_gather(x, axis, axis=0, tiled=True)  15.8 us
  transfers between devices with their start and end apart: 6, of which 6 were waited for; matrix products, arithmetic and copies ran while one was open for 1% of the time, Pallas kernels for 0%

commit v1 on v0

--- a/solution.py
+++ b/solution.py
@@ -7,6 +7,16 @@
 BLK = 128
 ROW = ("y", "c")
 COL = ("z", "x")
+
+
+def _write_column(shard_in, axis_key):
+    cards = []
+    for _ in range(lax.axis_size(axis_key)):
+        cards.append(shard_in)
+    upper = jnp.stack(cards)
+    mixed_arr = lax.all_to_all(upper, split_axis=0, axis_name=axis_key, concat_axis=0)
+    y = jnp.concatenate(mixed_arr, 0)
+    return y
 
 
 def widen(block_mask):
@@ -21,7 +31,7 @@
 
 def gather_rows(x, axes):
     for axis in reversed(axes):
-        x = lax.all_gather(x, axis, axis=0, tiled=True)
+        x = _write_column(x, axis)
     return x
 
 

time: 266 us -> 244 us (0.917)
  waiting for transfers between devices: 219 us -> 185 us
  starting transfers between devices: 0.21 us -> 15.9 us
  other arithmetic: 5.21 us -> 1.76 us
  local copies, waits for them, and re-layouts: 4.87 us -> 7.92 us
    all_gather x2 -> x0, waiting for transfers between devices: 82.5 us -> none  [gather_rows(): x = lax.all_gather(x, axis, axis=0, tiled=True)]
    all_to_all x0 -> x2, waiting for transfers between devices: none -> 54.2 us  [_write_column(): lax.all_to_all(upper, split_axis=0, axis_name=axis_key, concat_axis=0)]
    unnamed x6 -> x5, waiting for transfers between devices: 0.1 us -> 46.3 us
    reduce_scatter x1 -> x0, waiting for transfers between devices: 46 us -> none  [on_device(): summed = lax.psum_scatter(partial, 'y', scatter_dimension=0, tiled=True)]
    all_gather x2 -> x0, blocking collectives: 15.8 us -> none  [gather_rows(): x = lax.all_gather(x, axis, axis=0, tiled=True)]
    all_to_all x0 -> x2, starting transfers between devices: none -> 15.7 us  [_write_column(): lax.all_to_all(upper, split_axis=0, axis_name=axis_key, concat_axis=0)]
    all_to_all x0 -> x2, blocking collectives: none -> 14 us  [_write_column(): lax.all_to_all(upper, split_axis=0, axis_name=axis_key, concat_axis=0)]
    reduce_scatter x1, waiting for transfers between devices: 18.3 us -> 14.4 us  [on_device(): partial = lax.psum_scatter(partial, 'c', scatter_dimension=0, tiled=True)]
  transfers between devices with their start and end apart: 6 -> 6, of which waited for: 6 -> 6; matrix products, arithmetic and copies ran while one was open for 1% -> 0% of each run, Pallas kernels for 0% -> 0%
where the time goes in v1:
time: 244 us; the launch traced here: 243 us
  waiting for transfers between devices  185 us (76%)
  starting transfers between devices  15.9 us (7%)
  blocking collectives  14 us (6%)
  between operations  13.3 us (5%)
  local copies, waits for them, and re-layouts  7.92 us (3%)
  matrix products  5.31 us (2%)
    reduce_scatter x2, waiting for transfers between devices, on_device(): lax.psum_scatter(partial_out, axis, scatter_dimension=0, tiled=True)  70.4 us
    all_to_all x2, waiting for transfers between devices, _write_column(): lax.all_to_all(upper, split_axis=0, axis_name=axis_key, concat_axis=0)  54.2 us
    unnamed x5, waiting for transfers between devices  46.3 us
    all_to_all x2, starting transfers between devices, _write_column(): lax.all_to_all(upper, split_axis=0, axis_name=axis_key, concat_axis=0)  15.7 us
    reduce_scatter x1, waiting for transfers between devices, on_device(): partial = lax.psum_scatter(partial, 'c', scatter_dimension=0, tiled=True)  14.4 us
    all_to_all x2, blocking collectives, _write_column(): lax.all_to_all(upper, split_axis=0, axis_name=axis_key, concat_axis=0)  14 us
  transfers between devices with their start and end apart: 6, of which 6 were waited for; matrix products, arithmetic and copies ran while one was open for 0% of the time, Pallas kernels for 0%

profile of v1, /device:TPU:8, one launch (start us, length us, event | category | flops | bytes accessed | tf_op | source)
XLA Modules:
  0.0 243.4 jit_solution(12784983155712700515)
XLA Ops:
  6.5 0.8 stack.20
  7.3 10.1 %all_to_all.20 = bf16[4,32,512]{2,1,0:T(8,128)(2,1)S(1)} all-to-all(bf16[4,32,512]{2,1,0:T(8,128)(2,1)S(1)} %stack.20), channel_id=1, replica_groups=mesh['y'=8,'c'=2,'z'=8,'x'=4] {'x'}, dimensions={0} | all-to-all | bytes 262144 | tf_op jit(solution)/shard_map/all_to_all | solution.py:17
  17.4 1.1 stack.21
  18.5 10.3 %all-to-all-start.1 = ((bf16[8,128,512]{2,1,0:T(8,128)(2,1)}), bf16[8,128,512]{2,1,0:T(8,128)(2,1)S(1)}, u32[]{:S(2)}, u32[]{:S(2)}) async-start(bf16[8,128,512]{2,1,0:T(8,128)(2,1)} %stack.21), calls=%async_computation.1 | async-start | bytes 2097152 | tf_op jit(solution)/shard_map/all_to_all | solution.py:17
  28.9 0.2 broadcast_in_dim.6
  29.1 0.2 broadcast_in_dim.7
  29.3 0.2 bitcast_multiply_fusion.2
  29.5 26.6 %all-to-all-done.1 = bf16[8,128,512]{2,1,0:T(8,128)(2,1)S(1)} async-done(((bf16[8,128,512]{2,1,0:T(8,128)(2,1)}), bf16[8,128,512]{2,1,0:T(8,128)(2,1)S(1)}, u32[]{:S(2)}, u32[]{:S(2)}) %all-to-all-start.1) | async-done | bytes 1048608 | tf_op jit(solution)/shard_map/all_to_all | solution.py:17
  56.2 3.3 %convolution_bitcast_fusion = f32[1024,1024]{0,1:T(8,128)} fusion(bf16[1024,512]{1,0:T(8,128)(2,1)S(1)} %bitcast.32, bf16[512,512]{1,0:T(8,128)(2,1)S(1)} %get-tuple-element.7, bf16[512,512]{1,0:T(8,128)(2,1)S(1)} %get-tuple-element.8), kind=kOutput, calls=%fused_computation | convolution fusion | flops 1075838976 | bytes 6291456 | tf_op jit(solution)/shard_map/dot_general | solution.py:49
  59.5 14.4 %reduce-scatter.7.cloned.1.call-done = f32[512,1024]{0,1:T(8,128)} async-done(((f32[1024,1024]{0,1:T(8,128)}), f32[512,1024]{0,1:T(8,128)}) %reduce-scatter.7.cloned.1.call-update) | async-done | bytes 2097168 | tf_op jit(solution)/shard_map/reduce_scatter | solution.py:50
  74.0 2.9 %copy.13 = f32[512,1024]{1,0:T(8,128)} copy(f32[512,1024]{0,1:T(8,128)} %reduce-scatter.7.cloned.1.call-done) | data formatting | bytes 4194304
  76.9 46.2 %reduce-scatter.13.cloned.1.call-done = f32[64,1024]{1,0:T(8,128)} async-done(((f32[512,1024]{1,0:T(8,128)}), f32[64,1024]{1,0:T(8,128)}) %reduce-scatter.13.cloned.1.call-update) | async-done | bytes 262160
  123.1 1.0 fusion.7
  124.2 0.1 copy.16
  124.5 0.1 copy.12
  124.7 4.0 %all_to_all.21 = bf16[2,64,512]{2,1,0:T(8,128)(2,1)S(1)} all-to-all(bf16[2,64,512]{2,1,0:T(8,128)(2,1)S(1)} %copy.12), channel_id=1, replica_groups=mesh['y'=8,'c'=2,'z'=8,'x'=4] {'c'}, dimensions={0} | all-to-all | bytes 262144 | tf_op jit(solution)/shard_map/all_to_all | solution.py:17
  128.6 1.1 stack.24
  129.7 5.4 %all-to-all-start.3 = ((bf16[8,128,512]{2,1,0:T(8,128)(2,1)}), bf16[8,128,512]{2,1,0:T(8,128)(2,1)S(1)}, u32[]{:S(2)}, u32[]{:S(2)}) async-start(bf16[8,128,512]{2,1,0:T(8,128)(2,1)} %stack.24), calls=%async_computation.4 | async-start | bytes 2097152 | tf_op jit(solution)/shard_map/all_to_all | solution.py:17
  135.1 27.6 %all-to-all-done.3 = bf16[8,128,512]{2,1,0:T(8,128)(2,1)S(1)} async-done(((bf16[8,128,512]{2,1,0:T(8,128)(2,1)}), bf16[8,128,512]{2,1,0:T(8,128)(2,1)S(1)}, u32[]{:S(2)}, u32[]{:S(2)}) %all-to-all-start.3) | async-done | bytes 1048608 | tf_op jit(solution)/shard_map/all_to_all | solution.py:17
  162.7 0.2 broadcast_in_dim.8
  162.9 2.1 fusion.3
  165.1 43.2 %reduce-scatter.9.cloned.1.call-done = f32[128,512]{1,0:T(8,128)} async-done(((f32[1024,512]{1,0:T(8,128)}), f32[128,512]{1,0:T(8,128)}) %reduce-scatter.9.cloned.1.call-update) | async-done | bytes 262160 | tf_op jit(solution)/shard_map/reduce_scatter | solution.py:56
  208.3 27.1 %reduce-scatter.11.cloned.1.call-done = f32[32,512]{1,0:T(8,128)} async-done(((f32[128,512]{1,0:T(8,128)}), f32[32,512]{1,0:T(8,128)}) %reduce-scatter.11.cloned.1.call-update) | async-done | bytes 65552 | tf_op jit(solution)/shard_map/reduce_scatter | solution.py:56
  235.4 1.5 convert_element_type.34
  (27 shorter events, 0.6 us)
Async XLA Ops:
  6.5 22.3 %copy-start.3 = (s32[4,4]{1,0:T(4,128)S(1)}, s32[4,4]{1,0:T(4,128)}, u32[]{:S(2)}) copy-start(s32[4,4]{1,0:T(4,128)} %param.11) | copy-start | bytes 196
  6.5 22.3 %copy-start.4 = (s32[4,4]{1,0:T(4,128)S(1)}, s32[4,4]{1,0:T(4,128)}, u32[]{:S(2)}) copy-start(s32[4,4]{1,0:T(4,128)} %param.12) | copy-start | bytes 196
  17.4 11.9 %copy-start = (bf16[512,512]{1,0:T(8,128)(2,1)S(1)}, bf16[512,512]{1,0:T(8,128)(2,1)}, u32[]{:S(2)}) copy-start(bf16[512,512]{1,0:T(8,128)(2,1)} %param.9) | copy-start | bytes 1572868
  17.4 11.9 %copy-start.1 = (bf16[512,512]{1,0:T(8,128)(2,1)S(1)}, bf16[512,512]{1,0:T(8,128)(2,1)}, u32[]{:S(2)}) copy-start(bf16[512,512]{1,0:T(8,128)(2,1)} %param.8) | copy-start | bytes 1572868
  18.5 37.6 %all-to-all-start.1 = ((bf16[8,128,512]{2,1,0:T(8,128)(2,1)}), bf16[8,128,512]{2,1,0:T(8,128)(2,1)S(1)}, u32[]{:S(2)}, u32[]{:S(2)}) async-start(bf16[8,128,512]{2,1,0:T(8,128)(2,1)} %stack.21), calls=%async_computation.1 | async-start | bytes 2097152 | tf_op jit(solution)/shard_map/all_to_all | solution.py:17
  28.8 45.2 %reduce-scatter.7.cloned.1.call-start = ((), (), s32[]{:S(2)}) async-start(), calls=%async_computation.8 | async-start | bytes 6291456 | tf_op jit(solution)/shard_map/reduce_scatter | solution.py:50
  59.5 63.6 %reduce-scatter.13.cloned.1.call-start = ((), (), s32[]{:S(2)}) async-start(), calls=%async_computation.11 | async-start | bytes 2359296
  124.5 10.7 %copy-start.5 = (s32[4,4]{1,0:T(4,128)S(1)}, s32[4,4]{1,0:T(4,128)}, u32[]{:S(2)}) copy-start(s32[4,4]{1,0:T(4,128)} %param.13) | copy-start | bytes 196
  124.7 38.3 %copy-start.2 = (bf16[512,512]{1,0:T(8,128)(2,1)S(1)}, bf16[512,512]{1,0:T(8,128)(2,1)}, u32[]{:S(2)}) copy-start(bf16[512,512]{1,0:T(8,128)(2,1)} %param.10) | copy-start | bytes 1572868
  129.7 33.0 %all-to-all-start.3 = ((bf16[8,128,512]{2,1,0:T(8,128)(2,1)}), bf16[8,128,512]{2,1,0:T(8,128)(2,1)S(1)}, u32[]{:S(2)}, u32[]{:S(2)}) async-start(bf16[8,128,512]{2,1,0:T(8,128)(2,1)} %stack.24), calls=%async_computation.4 | async-start | bytes 2097152 | tf_op jit(solution)/shard_map/all_to_all | solution.py:17
  135.1 73.2 %reduce-scatter.9.cloned.1.call-start = ((), (), s32[]{:S(2)}) async-start(), calls=%async_computation.9 | async-start | bytes 2359296 | tf_op jit(solution)/shard_map/reduce_scatter | solution.py:56
  165.0 70.4 %reduce-scatter.11.cloned.1.call-start = ((), (), s32[]{:S(2)}) async-start(), calls=%async_computation.10 | async-start | bytes 327680 | tf_op jit(solution)/shard_map/reduce_scatter | solution.py:56
Sparse Core Ops, SparseCore 0:
  59.6 14.3 reduce-scatter.6
  77.0 46.0 reduce-scatter.12
  165.1 43.1 reduce-scatter.8
  211.0 24.4 reduce-scatter.10
